TPU v7x, 32 devices: a whole 2x2x4 slice. The times are simulated.
32 devices in a mesh: groups: 2 (over y), queue: 4 (over z), dp: 4 (over x, core).
Axes of the slice: x: 2, y: 2, z: 4, core: 2. Of those that a mesh axis runs over, the one named last changes fastest.
Arguments:
- query_inputs: bfloat16 [8192, 1024], P(('groups', 'queue', 'dp')), parts along dimension 0, may hold values from -30 to 30
- key_inputs: bfloat16 [512, 1024], P(('groups', 'queue', 'dp')), parts along dimension 0, may hold values from -6 to 6
- query_weight: bfloat16 [1024, 1024], replicated, may hold values from -4 to 4
- key_weight: bfloat16 [1024, 1024], replicated, may hold values from -0.1875 to 0.1875
- queue_keys: bfloat16 [2048, 1024], P(('groups', 'queue')), parts along dimension 0, may hold values from -2 to 2
- write_pointer: int32 [2], P('groups'), parts along dimension 0, may hold values from 0 to 255
- slot_owner: int32 [32], P('groups'), parts along dimension 0, may hold values from 0 to 15, each once
- positive_index: int32 [8192], P(('groups', 'queue', 'dp')), parts along dimension 0, may hold values from 0 to 1023
Outputs:
- loss: float32 [8192], P(('groups', 'queue', 'dp')), parts along dimension 0
- query_weight_grad: float32 [2048, 1024], P(('groups', 'queue', 'dp')), parts along dimension 0
- new_queue: bfloat16 [2048, 1024], P(('groups', 'queue')), parts along dimension 0
There are 2 independent parts, one for each index of `groups`. A program takes and returns all parts, laid end to end along the dimension named above; an argument that names none is the same for every part. Nothing has to cross between parts.
Inputs may be any that keep to these rules, and one draw needn't show every extreme that they name: slot_owner is a permutation of 0 to 15.
All inputs are finite; a program needn't handle non-finite values.
Results may differ from a plain program's by a relative error of at most 0.0075.
Values may be sent and summed in bfloat16 or wider, within the bound.
No kernel may reach another device: no remote copies, remote signals or barrier semaphores. Data moves between devices by JAX's collectives and lax.ppermute only.
A program may use at most 192 MiB of HBM per device.

v0:
```python
import jax
import jax.numpy as jnp
from jax import lax
from jax.sharding import PartitionSpec as P

temper = 0.05


def make_fold(units, mapped):

    def fold(carry, piece, start):
        top, total, mixture, chosen = carry
        scores = (
            lax.dot_general(
                units, piece, (((1,), (1,)), ((), ())), preferred_element_type=jnp.float32
            )
            / temper
        )
        new_top = jnp.maximum(top, jnp.max(scores, -1))
        expo = jnp.exp(scores - new_top[:, None])
        total = jnp.sum(expo, -1)
        mixture = jnp.dot(expo.astype(jnp.bfloat16), piece, preferred_element_type=jnp.float32)
        count = piece.shape[0]
        hit = (mapped >= 0) & (mapped < count)
        picked = jnp.take(piece, jnp.clip(mapped, 0, count - 1), axis=0).astype(jnp.float32)
        chosen = jnp.where(hit[:, None], picked, 0.0)
        return (new_top, total, mixture, chosen)

    return fold


def start_carry(count, width):
    return (
        jnp.full((count,), -1e30, jnp.float32),
        jnp.zeros((count,), jnp.float32),
        jnp.zeros((count, width), jnp.float32),
        jnp.zeros((count, width), jnp.float32),
    )


def body(
    query_inputs,
    key_inputs,
    query_weight,
    key_weight,
    queue_keys,
    write_pointer,
    slot_owner,
    positive_index,
):
    q_dev, width = query_inputs.shape
    k_dev = queue_keys.shape[0]
    new_dev = key_inputs.shape[0]
    n_dp = lax.axis_size("dp")
    query = jnp.dot(query_inputs, query_weight, preferred_element_type=jnp.float32)
    inv_len = lax.rsqrt(jnp.sum(query * query, -1, keepdims=True) + 1e-06)
    unit_f = query * inv_len
    unit = unit_f.astype(jnp.bfloat16)
    fold = make_fold(unit, positive_index)
    top, total, mixture, chosen = fold(
        start_carry(q_dev, width),
        lax.all_gather(queue_keys, "queue", axis=0, tiled=True),
        jnp.int32(0),
    )
    mixture = mixture / total[:, None]
    positive = jnp.sum(unit.astype(jnp.float32) * chosen, -1) / temper
    loss = top + jnp.log(total) - positive
    grad_unit = (mixture - chosen) / temper
    grad_query = (
        (grad_unit - unit_f * jnp.sum(unit_f * grad_unit, -1, keepdims=True)) * inv_len
    ).astype(jnp.bfloat16)
    n_all = lax.axis_size(("queue", "dp"))
    share = width // n_all
    term = lax.dot_general(
        query_inputs, grad_query, (((0,), (0,)), ((), ())), preferred_element_type=jnp.float32
    )
    summed = lax.psum(term, ("queue", "dp"))
    grad_rows = lax.dynamic_slice_in_dim(summed, lax.axis_index(("queue", "dp")) * share, share, 0)
    fresh = jnp.dot(key_inputs, key_weight, preferred_element_type=jnp.float32)
    fresh = (fresh * lax.rsqrt(jnp.sum(fresh * fresh, -1, keepdims=True) + 1e-06)).astype(
        jnp.bfloat16
    )
    arrived = lax.all_gather(fresh, ("queue", "dp"), axis=0, tiled=True)
    n_blocks = slot_owner.shape[0]
    slots_here = lax.axis_index("queue") * n_dp + jnp.arange(n_dp, dtype=jnp.int32)
    match = slot_owner[None, :] == slots_here[:, None]
    owner_block = jnp.sum(jnp.where(match, jnp.arange(n_blocks, dtype=jnp.int32)[None, :], 0), -1)
    offset = (jnp.arange(k_dev, dtype=jnp.int32) - write_pointer[0]) % k_dev
    live = offset < n_dp * new_dev
    sub_block = jnp.minimum(offset // new_dev, n_dp - 1)
    source = jnp.take(owner_block, sub_block) * new_dev + offset % new_dev
    new_queue = jnp.where(live[:, None], jnp.take(arrived, source, axis=0), queue_keys)
    return (loss, grad_rows, new_queue)


def solution(mesh):
    in_specs = (
        P(("groups", "queue", "dp"), None),
        P(("groups", "queue", "dp"), None),
        P(),
        P(),
        P(("groups", "queue"), None),
        P("groups"),
        P("groups"),
        P(("groups", "queue", "dp")),
    )
    out_specs = (
        P(("groups", "queue", "dp")),
        P(("groups", "queue", "dp"), None),
        P(("groups", "queue"), None),
    )
    return jax.shard_map(body, mesh=mesh, in_specs=in_specs, out_specs=out_specs, check_vma=False)
```

profile of v0, /device:TPU:0, one launch (start us, length us, event | category | flops | bytes accessed | tf_op | source)
XLA Modules:
  0.0 193.4 jit_solution(15796007540766359770)
XLA Ops:
  7.2 0.7 all-gather.2.cloned.1.call-update
  8.6 0.7 compare_select_fusion.9
  9.3 0.7 compare_and_fusion.1
  10.0 1.8 multiply_reduce_fusion.2
  11.9 46.1 %all-gather.2.cloned.1.call-done = bf16[1024,1024]{1,0:T(8,128)(2,1)} async-done(((bf16[256,1024]{1,0:T(8,128)(2,1)}), bf16[1024,1024]{1,0:T(8,128)(2,1)}) %all-gather.2.cloned.1.call-update) | async-done | bytes 2097168 | tf_op jit(solution)/shard_map/all_gather | solution.py:62
  58.0 2.4 %fusion.14 = (f32[256]{0:T(256)S(1)}, f32[256,1024]{1,0:T(8,128)S(1)}) fusion(bf16[1024,1024]{1,0:T(8,128)(2,1)} %all-gather.2.cloned.1.call-done, f32[256,1024]{1,0:T(8,128)S(1)} %get-tuple-element.23, f32[256]{0:T(256)S(1)} %add_rsqrt_fusion), kind=kOutput, calls=%fused_computation.68 | convolution fusion | flops 537919232 | bytes 4196352 | tf_op jit(solution)/shard_map/dot_general | solution.py:14
  60.4 1.0 copy-done.1
  61.4 0.3 fusion.3
  61.7 4.2 %gather_fusion = bf16[256,1024]{1,0:T(8,128)(2,1)} fusion(bf16[1024,1024]{1,0:T(8,128)(2,1)} %all-gather.2.cloned.1.call-done, s32[1024]{0:T(1024)S(1)} %pad_clamp_fusion.1), kind=kCustom, calls=%fused_computation | custom fusion | bytes 1049600 | tf_op jit(solution)/shard_map/jit(_take)/gather | solution.py:25
  65.9 3.1 %multiply_reduce_fusion = (f32[256]{0:T(256)S(1)}, f32[256]{0:T(256)S(1)}, f32[256,1024]{1,0:T(8,128)S(1)}) fusion(f32[256,1024]{1,0:T(8,128)S(1)} %get-tuple-element.23, f32[256]{0:T(256)S(1)} %add_rsqrt_fusion, bf16[256,1024]{1,0:T(8,128)(2,1)} %gather_fusion, pred[256]{0:T(512)(128)(4,1)S(1)} %get-tuple-element.16, ...), kind=kOutput, calls=%fused_computation.8 | convolution fusion | flops 540802560 | bytes 5772800 | tf_op jit(solution)/shard_map/dot_general | solution.py:22
  69.0 3.0 %convolution_bitcast_fusion = f32[1024,1024]{0,1:T(8,128)} fusion(bf16[256,1024]{1,0:T(8,128)(2,1)S(1)} %copy-done.2, f32[256,1024]{1,0:T(8,128)S(1)} %get-tuple-element.26, f32[256,1024]{1,0:T(8,128)S(1)} %get-tuple-element.23, f32[256]{0:T(256)S(1)} %get-tuple-element.12, f32[256]{0:T(256)S(1)} %add_rsqrt_fusion), kind=kOutput, calls=%fused_computation.2 | convolution fusion | flops 538181632 | bytes 6817792 | tf_op jit(solution)/shard_map/dot_general | solution.py:74
  72.0 0.6 copy-done.4
  72.6 0.2 select_reduce_fusion
  72.8 0.6 fusion.13
  73.4 2.5 %compare_select_fusion = (s32[256,1]{0,1:T(1,128)S(1)}, s32[256,1]{0,1:T(1,128)S(1)}) fusion(s32[]{:T(128)} %bitcast.16, s32[]{:T(128)} %bitcast.5, s32[]{:T(128)} %bitcast.4, s32[]{:T(128)} %bitcast.3, s32[]{:T(128)} %bitcast.2), kind=kLoop, calls=%fused_computation.23 | loop fusion | flops 12800 | bytes 2068 | tf_op jit(solution)/shard_map/jit(_take)/jit(_where)/select_n | solution.py:92
  76.0 2.2 %multiply_reduce_fusion.3 = (f32[16]{0:T(128)S(1)}, f32[16,1024]{1,0:T(8,128)S(1)}) fusion(bf16[16,1024]{1,0:T(8,128)(2,1)S(1)} %copy-done.3, bf16[1024,1024]{1,0:T(8,128)(2,1)} %param.11), kind=kOutput, calls=%fused_computation.22 | convolution fusion | flops 33587184 | bytes 2195520 | tf_op jit(solution)/shard_map/dot_general | solution.py:79
  78.2 0.1 multiply_convert_fusion.3
  78.3 23.5 %all_gather.7 = bf16[256,1024]{1,0:T(8,128)(2,1)S(1)} all-gather(bf16[16,1024]{1,0:T(8,128)(2,1)S(1)} %multiply_convert_fusion.3), channel_id=1, replica_groups=mesh['groups'=2,'queue'=4,'dp'=4] {'queue','dp'}, dimensions={0}, use_global_device_ids=true | all-gather | bytes 557056 | tf_op jit(solution)/shard_map/all_gather | solution.py:83
  101.8 1.2 gather_fusion.1
  103.0 2.0 %select_select_fusion = bf16[256,1024]{1,0:T(8,128)(2,1)} fusion(bf16[256,1024]{1,0:T(8,128)(2,1)} %param.12, bf16[256,1024]{1,0:T(8,128)(2,1)S(1)} %gather_fusion.1, pred[256]{0:T(512)(128)(4,1)S(1)} %get-tuple-element.29, pred[256]{0:T(512)(128)(4,1)S(1)} %get-tuple-element.30), kind=kLoop, calls=%fused_computation.16 | loop fusion | flops 524288 | bytes 1573376 | tf_op jit(solution)/shard_map/jit(_where)/select_n | solution.py:92
  105.0 0.6 multiply_subtract_fusion
  105.6 78.9 %all-reduce.2.cloned.1.call-done = f32[1024,1024]{0,1:T(8,128)} async-done(((f32[1024,1024]{0,1:T(8,128)}), f32[1024,1024]{0,1:T(8,128)}) %all-reduce.2.cloned.1.call-update) | async-done | bytes 4194320 | tf_op jit(solution)/shard_map/psum | solution.py:77
  184.5 1.2 constant_dynamic-slice_fusion
  185.7 0.9 copy.13
  (18 shorter events, 0.2 us)
Async XLA Ops:
  7.2 2.8 %copy-start = (bf16[1024,1024]{1,0:T(8,128)(2,1)S(1)}, bf16[1024,1024]{1,0:T(8,128)(2,1)}, u32[]{:S(2)}) copy-start(bf16[1024,1024]{1,0:T(8,128)(2,1)} %param.10) | copy-start | bytes 6291460
  7.2 50.8 %all-gather.2.cloned.1.call-start = ((), (), s32[]{:S(2)}) async-start(), calls=%async_computation | async-start | bytes 2621440 | tf_op jit(solution)/shard_map/all_gather | solution.py:62
  7.9 176.6 %all-reduce.2.cloned.1.call-start = ((), (), s32[]{:S(2)}) async-start(), calls=%async_computation.1 | async-start | bytes 8388608 | tf_op jit(solution)/shard_map/psum | solution.py:77
  60.4 1.0 copy-start.1
  65.9 3.1 %copy-start.2 = (bf16[256,1024]{1,0:T(8,128)(2,1)S(1)}, bf16[256,1024]{1,0:T(8,128)(2,1)}, u32[]{:S(2)}) copy-start(bf16[256,1024]{1,0:T(8,128)(2,1)} %param.8) | copy-start | bytes 1572868
  72.0 0.7 copy-start.4
  72.0 4.0 %copy-start.3 = (bf16[16,1024]{1,0:T(8,128)(2,1)S(1)}, bf16[16,1024]{1,0:T(8,128)(2,1)}, u32[]{:S(2)}) copy-start(bf16[16,1024]{1,0:T(8,128)(2,1)} %param.9) | copy-start | bytes 98308
Sparse Core Ops, SparseCore 0:
  9.6 48.3 all-gather.1
  72.1 112.3 all-reduce.1
where the time goes:
time: 194 us; the launch traced here: 193 us
  waiting for transfers between devices  126 us (65%)
  blocking collectives  23.5 us (12%)
  between operations  14.8 us (8%)
  matrix products  12.6 us (6%)
  local copies, waits for them, and re-layouts  9.73 us (5%)
  other arithmetic  7.09 us (4%)
    psum x1, waiting for transfers between devices, body(): summed = lax.psum(term, ('queue', 'dp'))  78.9 us
    all_gather x1, waiting for transfers between devices, body(): lax.all_gather(queue_keys, 'queue', axis=0, tiled=True)  46.1 us
    all_gather x1, blocking collectives, body(): arrived = lax.all_gather(fresh, ('queue', 'dp'), axis=0, tiled=True)  23.5 us
    gather x1, local copies, waits for them, and re-layouts, fold(): jnp.take(piece, jnp.clip(mapped, 0, count - 1), axis=0).astype(jnp.float32)  4.21 us
  transfers between devices with their start and end apart: 2, of which 2 were waited for; matrix products, arithmetic and copies ran while one was open for 7% of the time, Pallas kernels for 0%

commit v1 on v0

--- a/solution.py
+++ b/solution.py
@@ -74,7 +74,7 @@
     term = lax.dot_general(
         query_inputs, grad_query, (((0,), (0,)), ((), ())), preferred_element_type=jnp.float32
     )
-    summed = lax.psum(term, ("queue", "dp"))
+    summed = jnp.sum(lax.all_gather(term, ("queue", "dp")), axis=0)
     grad_rows = lax.dynamic_slice_in_dim(summed, lax.axis_index(("queue", "dp")) * share, share, 0)
     fresh = jnp.dot(key_inputs, key_weight, preferred_element_type=jnp.float32)
     fresh = (fresh * lax.rsqrt(jnp.sum(fresh * fresh, -1, keepdims=True) + 1e-06)).astype(

time: 194 us -> 500 us (2.58)
  waiting for transfers between devices: 126 us -> 343 us
  local copies, waits for them, and re-layouts: 9.73 us -> 75 us
  other arithmetic: 7.09 us -> 30.5 us
    all_gather x0 -> x1, waiting for transfers between devices: none -> 295 us  [body(): summed = jnp.sum(lax.all_gather(term, ('queue', 'dp')), axis=0)]
    psum x1 -> x0, waiting for transfers between devices: 78.9 us -> none  [body(): summed = lax.psum(term, ('queue', 'dp'))]
    unnamed x11 -> x12, local copies, waits for them, and re-layouts: 2.51 us -> 67.7 us
    reduce_sum x0 -> x1, other arithmetic: none -> 23.4 us  [body(): summed = jnp.sum(lax.all_gather(term, ('queue', 'dp')), axis=0)]
  transfers between devices with their start and end apart: 2 -> 2, of which waited for: 2 -> 2; matrix products, arithmetic and copies ran while one was open for 7% -> 3% of each run, Pallas kernels for 0% -> 0%
where the time goes in v1:
time: 500 us; the launch traced here: 499 us
  waiting for transfers between devices  343 us (69%)
  local copies, waits for them, and re-layouts  75 us (15%)
  other arithmetic  30.5 us (6%)
  blocking collectives  23.7 us (5%)
  between operations  14.8 us (3%)
  matrix products  12.6 us (3%)
    all_gather x1, waiting for transfers between devices, body(): summed = jnp.sum(lax.all_gather(term, ('queue', 'dp')), axis=0)  295 us
    unnamed x12, local copies, waits for them, and re-layouts  67.7 us
    all_gather x1, waiting for transfers between devices, body(): lax.all_gather(queue_keys, 'queue', axis=0, tiled=True)  46.8 us
    all_gather x1, blocking collectives, body(): arrived = lax.all_gather(fresh, ('queue', 'dp'), axis=0, tiled=True)  23.7 us
    reduce_sum x1, other arithmetic, body(): summed = jnp.sum(lax.all_gather(term, ('queue', 'dp')), axis=0)  23.4 us
  transfers between devices with their start and end apart: 2, of which 2 were waited for; matrix products, arithmetic and copies ran while one was open for 3% of the time, Pallas kernels for 0%

profile of v1, /device:TPU:0, one launch (start us, length us, event | category | flops | bytes accessed | tf_op | source)
XLA Modules:
  0.0 499.4 jit_solution(13609010783588823303)
XLA Ops:
  7.2 0.7 all-gather.4.cloned.1.call-update
  8.0 0.7 compare_select_fusion.9
  8.7 0.7 compare_and_fusion.1
  9.3 1.8 multiply_reduce_fusion.2
  11.2 46.8 %all-gather.4.cloned.1.call-done = bf16[1024,1024]{1,0:T(8,128)(2,1)} async-done(((bf16[256,1024]{1,0:T(8,128)(2,1)}), bf16[1024,1024]{1,0:T(8,128)(2,1)}) %all-gather.4.cloned.1.call-update) | async-done | bytes 2097168 | tf_op jit(solution)/shard_map/all_gather | solution.py:62
  58.0 2.4 fusion.14
  60.4 1.0 copy-done.1
  61.4 0.3 fusion.3
  61.7 4.2 gather_fusion
  65.9 3.1 multiply_reduce_fusion
  69.0 3.0 convolution_bitcast_fusion
  72.7 0.2 select_reduce_fusion
  72.9 0.7 fusion.13
  73.5 2.6 compare_select_fusion
  76.1 2.2 multiply_reduce_fusion.3
  78.5 23.7 %all_gather.15 = bf16[256,1024]{1,0:T(8,128)(2,1)S(1)} all-gather(bf16[16,1024]{1,0:T(8,128)(2,1)S(1)} %multiply_convert_fusion.3), channel_id=1, replica_groups=mesh['groups'=2,'queue'=4,'dp'=4] {'queue','dp'}, dimensions={0}, use_global_device_ids=true | all-gather | bytes 557056 | tf_op jit(solution)/shard_map/all_gather | solution.py:83
  102.1 1.2 gather_fusion.1
  103.3 2.0 select_select_fusion
  105.3 0.6 multiply_subtract_fusion
  105.9 295.3 %all-gather.6.cloned.1.call-done = f32[16384,1024]{0,1:T(8,128)} async-done(((f32[1024,1024]{0,1:T(8,128)}), f32[16384,1024]{0,1:T(8,128)}) %all-gather.6.cloned.1.call-update) | async-done | bytes 67108880 | tf_op jit(solution)/shard_map/all_gather | solution.py:77
  401.2 65.8 %copy.13 = f32[128,8,16,1024]{3,2,1,0:T(8,128)} copy(f32[128,8,16,1024]{3,1,2,0:T(8,128)} %bitcast.9) | data formatting | bytes 134217728
  467.1 23.4 %bitcast_reduce_fusion = f32[1024,1024]{0,1:T(8,128)} fusion(f32[128,8,16,1024]{3,2,1,0:T(8,128)} %copy.13), kind=kLoop, calls=%fused_computation.2 | loop fusion | flops 15728640 | bytes 71303168 | tf_op jit(solution)/shard_map/reduce_sum | solution.py:77
  490.4 1.2 constant_dynamic-slice_fusion
  491.7 0.9 copy.12
  (20 shorter events, 0.3 us)
Async XLA Ops:
  7.2 2.2 copy-start
  7.2 50.8 %all-gather.4.cloned.1.call-start = ((), (), s32[]{:S(2)}) async-start(), calls=%async_computation | async-start | bytes 2621440 | tf_op jit(solution)/shard_map/all_gather | solution.py:62
  7.9 393.3 %all-gather.6.cloned.1.call-start = ((), (), s32[]{:S(2)}) async-start(), calls=%async_computation.1 | async-start | bytes 71303168 | tf_op jit(solution)/shard_map/all_gather | solution.py:77
  60.4 1.0 copy-start.1
  65.9 3.1 copy-start.2
  72.0 0.7 copy-start.4
  72.0 4.2 copy-start.3
Sparse Core Ops, SparseCore 0:
  9.6 48.3 all-gather.3
  72.1 329.0 all-gather.5
